TPU v7x, 32 devices: a whole 2x2x4 slice. The times are simulated.
32 devices in a mesh: energy: 4 (over z), atom: 8 (over y, x, core).
Axes of the slice: x: 2, y: 2, z: 4, core: 2. Of those that a mesh axis runs over, the one named last changes fastest.
Arguments:
- t_mats: bfloat16 [4, 16, 2048], P('energy', 'atom'), may hold values from -0.75 to 0.75
- struct_table: bfloat16 [4, 64, 2048], P('energy'), may hold values from -0.359375 to 0.359375
- zone_atoms: int32 [16, 64], P('atom'), may hold values from 0 to 15, as said below
- zone_size: int32 [16], P('atom'), may hold values from 32 to 64
- pair_index: int32 [16, 384], P('atom'), may hold values from 0 to 63
- zone_link: int32 [16, 384], P('atom'), may hold values from 0 to 63
- weights: float32 [4, 2], P('energy'), may hold values from -1 to 1
Outputs:
- green: float32 [16, 2048], P('atom')
Inputs may be any that keep to these rules, and one draw needn't show every extreme that they name: Atom g is owned by index g // 2 of the atom axis; zone_atoms[g, 0] is g; the owner of every member of atom g's zone lies -4 to 3 steps from g's owner along the atom axis, counted around the axis, and both extreme offsets occur in every zone; members may repeat (periodic images).
All inputs are finite; a program needn't handle non-finite values.
Results may differ from a plain program's by a relative error of at most 0.003.
Values may be sent and summed in bfloat16 or wider, within the bound.
No kernel may reach another device: no remote copies, remote signals or barrier semaphores. Data moves between devices by JAX's collectives and lax.ppermute only.
A program may use at most 128 MiB of HBM per device.

v0:
```python
import jax
import jax.numpy as jnp
from jax import lax
from jax.sharding import PartitionSpec as P

L = 32
Z = 64
NB = 6


def real_form(block):
    parts = block.reshape(block.shape[:-1] + (2, L, L))
    real_part = parts[..., 0, :, :]
    imag_part = parts[..., 1, :, :]
    top_rows = jnp.concatenate([real_part, -imag_part], axis=-1)
    bottom_rows = jnp.concatenate([imag_part, real_part], axis=-1)
    return jnp.concatenate([top_rows, bottom_rows], axis=-2)


def take_rows(table, index):
    a_dev = index.shape[0]
    return jnp.take_along_axis(table, index.reshape(a_dev, -1), axis=1).reshape(index.shape)


def body(t_mats, struct_table, zone_atoms, zone_size, pair_index, zone_link, weights):
    e_dev, a_dev, block_flat = t_mats.shape
    window = lax.all_gather(t_mats, "atom", axis=1, tiled=True)
    coupling = jnp.arange(NB, dtype=jnp.int32)
    s2 = zone_link[:, :NB]
    s1 = take_rows(zone_link, s2[:, :, None] * NB + coupling)
    n1 = NB * NB
    slots = jnp.concatenate([s1.reshape(a_dev, n1), s2, jnp.zeros((a_dev, 1), jnp.int32)], axis=1)
    spots = slots[:, :, None] * NB + coupling
    pairs = take_rows(pair_index, spots)
    links = take_rows(zone_link, spots)
    members = take_rows(zone_atoms, slots)
    present = slots < zone_size[:, None]
    t_block = jnp.where(present[None, :, :, None], window[:, members], jnp.zeros((), jnp.bfloat16))
    t_real = real_form(t_block)
    g_real = real_form(struct_table[:, pairs])
    start_b = real_form(t_mats)[..., :L]
    start_f = start_b.astype(jnp.float32)
    is_zero = (slots == 0)[None, :, :, None, None]
    p1 = jnp.einsum(
        "easkij,eajc->easkic", g_real[:, :, :n1], start_b, preferred_element_type=jnp.float32
    )
    hit = (links[:, :n1] == 0)[None, :, :, :, None, None]
    coupled1 = jnp.sum(jnp.where(hit, p1, 0.0), axis=3).astype(jnp.bfloat16)
    col1 = jnp.einsum(
        "easij,easjc->easic", t_real[:, :, :n1], coupled1, preferred_element_type=jnp.float32
    ) + jnp.where(is_zero[:, :, :n1], start_f[:, :, None], 0.0)
    near2 = col1.astype(jnp.bfloat16).reshape(e_dev, a_dev, NB, NB, 2 * L, L)
    g2 = g_real[:, :, n1 : n1 + NB]
    coupled2 = jnp.einsum(
        "eamnij,eamnjc->eamic", g2, near2, preferred_element_type=jnp.float32
    ).astype(jnp.bfloat16)
    col2 = jnp.einsum(
        "eamij,eamjc->eamic",
        t_real[:, :, n1 : n1 + NB],
        coupled2,
        preferred_element_type=jnp.float32,
    ) + jnp.where(is_zero[:, :, n1 : n1 + NB], start_f[:, :, None], 0.0)
    near3 = col2.astype(jnp.bfloat16)
    coupled3 = jnp.einsum(
        "eanij,eanjc->eaic", g_real[:, :, n1 + NB], near3, preferred_element_type=jnp.float32
    ).astype(jnp.bfloat16)
    diagonal = (
        jnp.einsum(
            "eaij,eajc->eaic", t_real[:, :, n1 + NB], coupled3, preferred_element_type=jnp.float32
        )
        + start_f
    )
    real_rows = diagonal[:, :, :L, :].reshape(e_dev, a_dev, L * L)
    imag_rows = diagonal[:, :, L:, :].reshape(e_dev, a_dev, L * L)
    w_real = weights[:, 0][:, None, None]
    w_imag = weights[:, 1][:, None, None]
    green_real = jnp.sum(w_real * real_rows - w_imag * imag_rows, axis=0)
    green_imag = jnp.sum(w_real * imag_rows + w_imag * real_rows, axis=0)
    local_green = jnp.concatenate([green_real, green_imag], axis=-1)
    return lax.psum(local_green, "energy")


def solution(mesh):
    return jax.shard_map(
        body,
        mesh=mesh,
        in_specs=(
            P("energy", "atom", None),
            P("energy", None, None),
            P("atom", None),
            P("atom"),
            P("atom", None),
            P("atom", None),
            P("energy", None),
        ),
        out_specs=P("atom", None),
        check_vma=False,
    )
```

profile of v0, /device:TPU:0, one launch (start us, length us, event | category | flops | bytes accessed | tf_op | source)
XLA Modules:
  0.0 100.4 jit_solution(1606972806575443180)
XLA Ops:
  0.0 0.8 slice_bitcast_fusion.6
  1.1 2.2 %gather_fusion.2 = s32[72]{0:T(128)S(1)} fusion(s32[2,384]{1,0:T(2,128)} %param.14, s32[72]{0:T(128)S(1)} %reshape.652), kind=kCustom, calls=%fused_computation.4 | custom fusion | bytes 1152 | tf_op jit(solution)/shard_map/jit(take_along_axis)/gather | solution.py:22
  3.7 0.1 add.215
  3.9 0.1 add.217
  4.1 9.7 %gather_fusion.4 = s32[516]{0:T(1024)S(1)} fusion(s32[2,384]{1,0:T(2,128)} %param.13, s32[516]{0:T(1024)S(1)} %reshape.682), kind=kCustom, calls=%fused_computation.clone | custom fusion | bytes 8256 | tf_op jit(solution)/shard_map/jit(take_along_axis)/gather | solution.py:22
  13.9 7.5 %gather_fusion.5 = s32[516]{0:T(1024)S(1)} fusion(s32[2,384]{1,0:T(2,128)S(1)} %copy-done.1, s32[516]{0:T(1024)S(1)} %reshape.682), kind=kCustom, calls=%fused_computation.1.clone | custom fusion | bytes 8256 | tf_op jit(solution)/shard_map/jit(take_along_axis)/gather | solution.py:22
  21.6 0.1 reshape.614
  21.7 0.1 reshape.608
  21.8 0.1 reshape.646
  22.0 3.4 %gather_fusion.1 = bf16[516,2048]{1,0:T(8,128)(2,1)S(1)} fusion(bf16[64,2048]{1,0:T(8,128)(2,1)S(1)} %bitcast.108, s32[1024]{0:T(1024)S(1)} %pad_clamp_fusion), kind=kCustom, calls=%fused_computation.3 | custom fusion | bytes 4229136 | tf_op jit(solution)/shard_map/gather | solution.py:40
  25.4 9.3 %reshape.609 = bf16[1,2,43,6,2,32,32]{6,5,4,3,2,1,0:T(8,128)(2,1)} reshape(bf16[516,2048]{1,0:T(8,128)(2,1)S(1)} %gather_fusion.1) | data formatting | bytes 4227072 | tf_op jit(solution)/shard_map/reshape | solution.py:12
  34.7 7.3 %slice_bitcast_fusion = (bf16[1,2,43,6,32,32]{5,4,3,2,1,0:T(8,128)(2,1)}, bf16[1,2,43,6,32,32]{5,4,3,2,1,0:T(8,128)(2,1)}) fusion(bf16[1,2,43,6,2,32,32]{6,5,4,3,2,1,0:T(8,128)(2,1)} %reshape.609), kind=kLoop, calls=%fused_computation.14 | loop fusion | bytes 4227072 | tf_op jit(solution)/shard_map/squeeze | solution.py:14
  42.1 1.5 %copy-done.3 = bf16[1,2,43,6,2,32,32]{6,5,4,3,2,1,0:T(8,128)(2,1)S(1)} copy-done((bf16[1,2,43,6,2,32,32]{6,5,4,3,2,1,0:T(8,128)(2,1)S(1)}, bf16[1,2,43,6,2,32,32]{6,5,4,3,2,1,0:T(8,128)(2,1)}, u32[]{:S(2)}) %copy-start.3) | copy-done | bytes 2113560
  43.6 2.5 %fusion.70 = bf16[1,2,43,6,32,32]{5,4,3,2,1,0:T(8,128)(2,1)} fusion(bf16[1,2,43,6,2,32,32]{6,5,4,3,2,1,0:T(8,128)(2,1)S(1)} %copy-done.3), kind=kLoop, calls=%fused_computation.115 | loop fusion | flops 528384 | bytes 2113536 | tf_op jit(solution)/shard_map/neg | solution.py:15
  46.5 9.5 %select_reduce_fusion = bf16[2,36,64,32]{2,3,1,0:T(8,128)(2,1)S(1)} fusion(pred[2,36,6]{2,1,0:T(8,128)(4,1)S(1)} %slice_compare_fusion, bf16[1,2,43,6,32,32]{5,4,3,2,1,0:T(8,128)(2,1)} %get-tuple-element.13, bf16[1,2,43,6,32,32]{5,4,3,2,1,0:T(8,128)(2,1)} %get-tuple-element.12, bf16[1,2,43,6,32,32]{5,4,3,2,1,0:T(8,128)(2,1)} %fusion.70, ...), kind=kOutput, calls=%fused_computation.13 | convolution fusion | flops 129024000 | bytes 3473840 | tf_op jit(solution)/shard_map/easkij,eajc->easkic/dot_general | solution.py:44
  56.2 2.0 %gather_fusion.3 = s32[86]{0:T(128)S(1)} fusion(s32[2,64]{1,0:T(2,128)S(1)} %copy-done.2, s32[86]{0:T(128)S(1)} %reshape.658), kind=kCustom, calls=%fused_computation.5 | custom fusion | bytes 1376 | tf_op jit(solution)/shard_map/jit(take_along_axis)/gather | solution.py:22
  58.4 10.7 %all_gather.3 = bf16[1,16,2048]{2,0,1:T(2,128)(2,1)S(1)} all-gather(bf16[1,2,2048]{2,0,1:T(2,128)(2,1)S(1)} %copy.27), channel_id=1, replica_groups=mesh['energy'=4,'atom'=8] {'atom'}, dimensions={1}, use_global_device_ids=true | all-gather | bytes 73728 | tf_op jit(solution)/shard_map/all_gather | solution.py:27
  69.1 0.8 gather_fusion
  69.9 1.1 %reshape.694 = bf16[1,2,43,2,32,32]{5,4,3,2,1,0:T(8,128)(2,1)S(1)} reshape(bf16[86,2048]{1,0:T(8,128)(2,1)S(1)} %gather_fusion) | data formatting | bytes 704512 | tf_op jit(solution)/shard_map/gather | solution.py:38
  71.1 0.2 copy_select_fusion
  71.3 0.3 slice_bitcast_fusion.2
  71.6 0.1 fusion.69
  71.8 0.9 fusion.8
  72.8 0.6 copy-done.5
  73.3 1.3 %slice-done.1 = s8[4194304]{0:T(1024)(128)(4,1)S(1)} async-done(((s8[4227072]{0:T(1024)(128)(4,1)}), s8[4194304]{0:T(1024)(128)(4,1)S(1)}, s32[]{:S(2)}) %slice-start.1) | async-done | bytes 4194328
  74.7 1.3 %copy-done.4 = bf16[1,2,43,6,32,32]{5,4,3,2,1,0:T(8,128)(2,1)S(1)} copy-done((bf16[1,2,43,6,32,32]{5,4,3,2,1,0:T(8,128)(2,1)S(1)}, bf16[1,2,43,6,32,32]{5,4,3,2,1,0:T(8,128)(2,1)}, u32[]{:S(2)}) %copy-start.4) | copy-done | bytes 1056792
  75.9 0.8 fusion.23
  76.8 1.5 %fusion.27 = bf16[2,64,32]{1,2,0:T(8,128)(2,1)S(1)} fusion(bf16[2,6,64,32]{2,3,1,0:T(8,128)(2,1)S(1)} %fusion.23, bf16[1,2,43,32,32]{4,3,2,1,0:T(8,128)(2,1)S(1)} %get-tuple-element.15, bf16[1,2,43,32,32]{4,3,2,1,0:T(8,128)(2,1)S(1)} %get-tuple-element.14, bf16[1,2,43,32,32]{4,3,2,1,0:T(8,128)(2,1)S(1)} %fusion.69, ...), kind=kOutput, calls=%fused_computation.41 | convolution fusion | flops 7155712 | bytes 3772428 | tf_op jit(solution)/shard_map/eanij,eanjc->eaic/dot_general | solution.py:64
  78.2 0.2 fusion.26
  78.5 0.6 fusion.73
  79.1 1.4 %multiply_subtract_fusion = (f32[1,2,32,32]{2,3,1,0:T(8,128)S(1)}, f32[1,2,32,32]{2,3,1,0:T(8,128)S(1)}) fusion(f32[1,2,64,32]{2,3,1,0:T(8,128)S(1)} %fusion.26, f32[]{:T(128)} %bitcast.32, f32[]{:T(128)} %bitcast), kind=kLoop, calls=%fused_computation.75 | loop fusion | flops 12288 | bytes 32776 | tf_op jit(solution)/shard_map/sub | solution.py:77
  80.8 19.6 %psum.7 = f32[2,2048]{1,0:T(2,128)} all-reduce(f32[2,2048]{1,0:T(2,128)S(1)} %pad_maximum_fusion.8), channel_id=1, replica_groups=mesh['energy'=4,'atom'=8] {'energy'}, use_global_device_ids=true, to_apply=%region_1.0 | all-reduce | flops 4096 | bytes 32768 | tf_op jit(solution)/shard_map/psum | solution.py:80
  (64 shorter events, 2.4 us)
Async XLA Ops:
  0.0 22.0 %copy-start = (bf16[1,64,2048]{2,1,0:T(8,128)(2,1)S(1)}, bf16[1,64,2048]{2,1,0:T(8,128)(2,1)}, u32[]{:S(2)}) copy-start(bf16[1,64,2048]{2,1,0:T(8,128)(2,1)} %param.10) | copy-start | bytes 786436
  0.0 13.9 %copy-start.1 = (s32[2,384]{1,0:T(2,128)S(1)}, s32[2,384]{1,0:T(2,128)}, u32[]{:S(2)}) copy-start(s32[2,384]{1,0:T(2,128)} %param.14) | copy-start | bytes 9220
  34.7 8.9 %copy-start.3 = (bf16[1,2,43,6,2,32,32]{6,5,4,3,2,1,0:T(8,128)(2,1)S(1)}, bf16[1,2,43,6,2,32,32]{6,5,4,3,2,1,0:T(8,128)(2,1)}, u32[]{:S(2)}) copy-start(bf16[1,2,43,6,2,32,32]{6,5,4,3,2,1,0:T(8,128)(2,1)} %reshape.609) | copy-start | bytes 6340612
  43.6 2.5 %copy-start.6 = (bf16[1,2,2048]{2,1,0:T(2,128)(2,1)S(1)}, bf16[1,2,2048]{2,1,0:T(2,128)(2,1)}, u32[]{:S(2)}) copy-start(bf16[1,2,2048]{2,1,0:T(2,128)(2,1)} %param.9) | copy-start | bytes 24580
  46.5 9.7 %copy-start.2 = (s32[2,64]{1,0:T(2,128)S(1)}, s32[2,64]{1,0:T(2,128)}, u32[]{:S(2)}) copy-start(s32[2,64]{1,0:T(2,128)} %param.11) | copy-start | bytes 1540
  56.0 15.1 %copy-start.8 = (s32[2]{0:T(128)S(1)}, s32[2]{0:T(128)}, u32[]{:S(2)}) copy-start(s32[2]{0:T(128)} %param.12) | copy-start | bytes 28
  69.9 2.8 %slice-start = ((s8[4227072]{0:T(1024)(128)(4,1)}), s8[32768]{0:T(1024)(128)(4,1)S(1)}, s32[]{:S(2)}) async-start(s8[4227072]{0:T(1024)(128)(4,1)} %bitcast.110), calls=%async_computation | async-start | bytes 65536
  71.1 2.2 %copy-start.5 = (bf16[1,2,43,6,32,32]{5,4,3,2,1,0:T(8,128)(2,1)S(1)}, bf16[1,2,43,6,32,32]{5,4,3,2,1,0:T(8,128)(2,1)}, u32[]{:S(2)}) copy-start(bf16[1,2,43,6,32,32]{5,4,3,2,1,0:T(8,128)(2,1)} %get-tuple-element.13) | copy-start | bytes 3170308
  71.3 3.3 %slice-start.1 = ((s8[4227072]{0:T(1024)(128)(4,1)}), s8[4194304]{0:T(1024)(128)(4,1)S(1)}, s32[]{:S(2)}) async-start(s8[4227072]{0:T(1024)(128)(4,1)} %bitcast.110), calls=%async_computation.1 | async-start | bytes 8388608
  71.6 4.3 %copy-start.4 = (bf16[1,2,43,6,32,32]{5,4,3,2,1,0:T(8,128)(2,1)S(1)}, bf16[1,2,43,6,32,32]{5,4,3,2,1,0:T(8,128)(2,1)}, u32[]{:S(2)}) copy-start(bf16[1,2,43,6,32,32]{5,4,3,2,1,0:T(8,128)(2,1)} %get-tuple-element.12) | copy-start | bytes 3170308
  76.8 1.7 %copy-start.7 = (f32[1,2]{1,0:T(1,128)S(1)}, f32[1,2]{1,0:T(1,128)}, u32[]{:S(2)}) copy-start(f32[1,2]{1,0:T(1,128)} %param.15) | copy-start | bytes 28
where the time goes:
time: 101 us; the launch traced here: 100 us
  local copies, waits for them, and re-layouts  51.6 us (51%)
  blocking collectives  30.3 us (30%)
  matrix products  12.9 us (13%)
  other arithmetic  5.4 us (5%)
    gather x11, local copies, waits for them, and re-layouts, take_rows(): jnp.take_along_axis(table, index.reshape(a_dev, -1), axis=1)  22.1 us
    psum x1, blocking collectives, body(): return lax.psum(local_green, 'energy')  19.6 us
    all_gather x1, blocking collectives, body(): window = lax.all_gather(t_mats, 'atom', axis=1, tiled=True)  10.7 us
    dot_general x1, matrix products, body(): jnp.einsum('easkij,eajc->easkic', g_real[:, :, :n1], start_b, preferred_e...  9.49 us
    reshape x2, local copies, waits for them, and re-layouts, real_form(): parts = block.reshape(block.shape[:-1] + (2, L, L))  9.42 us
    squeeze x2, local copies, waits for them, and re-layouts, real_form(): imag_part = parts[..., 1, :, :]  7.6 us
    unnamed x26, local copies, waits for them, and re-layouts  4.99 us
    gather x1, local copies, waits for them, and re-layouts, body(): g_real = real_form(struct_table[:, pairs])  3.39 us

commit v1 on v0

--- a/solution.py
+++ b/solution.py
@@ -24,7 +24,14 @@
 
 def body(t_mats, struct_table, zone_atoms, zone_size, pair_index, zone_link, weights):
     e_dev, a_dev, block_flat = t_mats.shape
-    window = lax.all_gather(t_mats, "atom", axis=1, tiled=True)
+    count = lax.axis_size("atom")
+    route = [(i, (i + 1) % count) for i in range(count)]
+    pieces = [t_mats]
+    for far in range(1, count):
+        pieces = [lax.ppermute(pieces[0], "atom", route), *pieces]
+    full = jnp.concatenate(pieces, axis=1)
+    shift = (lax.axis_index("atom") + 1) * pieces[-1].shape[1]
+    window = jnp.roll(full, shift, axis=1)
     coupling = jnp.arange(NB, dtype=jnp.int32)
     s2 = zone_link[:, :NB]
     s1 = take_rows(zone_link, s2[:, :, None] * NB + coupling)

time: 101 us -> 114 us (1.13)
  waiting for transfers between devices: 0 us -> 20.6 us
  blocking collectives: 30.3 us -> 20.3 us
  starting transfers between devices: 0 us -> 3.12 us
  local copies, waits for them, and re-layouts: 51.6 us -> 49.4 us
  matrix products: 12.9 us -> 14.4 us
    ppermute x0 -> x7, waiting for transfers between devices: none -> 20.6 us  [body(): pieces = [lax.ppermute(pieces[0], 'atom', route), *pieces]]
    all_gather x1 -> x0, blocking collectives: 10.7 us -> none  [body(): window = lax.all_gather(t_mats, 'atom', axis=1, tiled=True)]
    ppermute x0 -> x7, starting transfers between devices: none -> 3.12 us  [body(): pieces = [lax.ppermute(pieces[0], 'atom', route), *pieces]]
    unnamed x26 -> x20, local copies, waits for them, and re-layouts: 4.99 us -> 2.59 us
    dot_general x1, matrix products: 0.75 us -> 2.17 us  [body(): jnp.einsum('eamnij,eamnjc->eamic', g2, near2, preferred_element_type=jnp....]
  transfers between devices with their start and end apart: 0 -> 7, of which waited for: 0 -> 6; matrix products, arithmetic and copies ran while one was open for 0% -> 51% of each run, Pallas kernels for 0% -> 0%
where the time goes in v1:
time: 114 us; the launch traced here: 113 us
  local copies, waits for them, and re-layouts  49.4 us (43%)
  waiting for transfers between devices  20.6 us (18%)
  blocking collectives  20.3 us (18%)
  matrix products  14.4 us (13%)
  other arithmetic  5.23 us (5%)
  starting transfers between devices  3.12 us (3%)
    gather x11, local copies, waits for them, and re-layouts, take_rows(): jnp.take_along_axis(table, index.reshape(a_dev, -1), axis=1)  22.1 us
    ppermute x7, waiting for transfers between devices, body(): pieces = [lax.ppermute(pieces[0], 'atom', route), *pieces]  20.6 us
    psum x1, blocking collectives, body(): return lax.psum(local_green, 'energy')  20.3 us
    dot_general x1, matrix products, body(): jnp.einsum('easkij,eajc->easkic', g_real[:, :, :n1], start_b, preferred_e...  9.58 us
    reshape x2, local copies, waits for them, and re-layouts, real_form(): parts = block.reshape(block.shape[:-1] + (2, L, L))  9.45 us
    squeeze x2, local copies, waits for them, and re-layouts, real_form(): imag_part = parts[..., 1, :, :]  7.6 us
    gather x1, local copies, waits for them, and re-layouts, body(): g_real = real_form(struct_table[:, pairs])  3.39 us
    ppermute x7, starting transfers between devices, body(): pieces = [lax.ppermute(pieces[0], 'atom', route), *pieces]  3.12 us
  transfers between devices with their start and end apart: 7, of which 6 were waited for; matrix products, arithmetic and copies ran while one was open for 51% of the time, Pallas kernels for 0%

profile of v1, /device:TPU:0, one launch (start us, length us, event | category | flops | bytes accessed | tf_op | source)
XLA Modules:
  0.0 113.4 jit_solution(326409212958447830)
XLA Ops:
  0.0 0.5 collective-permute-start
  0.5 0.7 slice_bitcast_fusion.6
  1.6 2.2 %gather_fusion.2 = s32[72]{0:T(128)S(1)} fusion(s32[2,384]{1,0:T(2,128)} %param.14, s32[72]{0:T(128)S(1)} %reshape.652), kind=kCustom, calls=%fused_computation.4 | custom fusion | bytes 1152 | tf_op jit(solution)/shard_map/jit(take_along_axis)/gather | solution.py:22
  4.5 9.7 %gather_fusion.5 = s32[516]{0:T(1024)S(1)} fusion(s32[2,384]{1,0:T(2,128)} %param.14, s32[516]{0:T(1024)S(1)} %reshape.682), kind=kCustom, calls=%fused_computation.1.clone | custom fusion | bytes 8256 | tf_op jit(solution)/shard_map/jit(take_along_axis)/gather | solution.py:22
  14.2 7.5 %gather_fusion.4 = s32[516]{0:T(1024)S(1)} fusion(s32[2,384]{1,0:T(2,128)S(1)} %copy-done.1, s32[516]{0:T(1024)S(1)} %reshape.682), kind=kCustom, calls=%fused_computation.clone | custom fusion | bytes 8256 | tf_op jit(solution)/shard_map/jit(take_along_axis)/gather | solution.py:22
  22.1 3.4 %gather_fusion.1 = bf16[516,2048]{1,0:T(8,128)(2,1)S(1)} fusion(bf16[64,2048]{1,0:T(8,128)(2,1)S(1)} %bitcast.107, s32[1024]{0:T(1024)S(1)} %pad_clamp_fusion), kind=kCustom, calls=%fused_computation.3 | custom fusion | bytes 4229136 | tf_op jit(solution)/shard_map/gather | solution.py:47
  25.5 9.4 %reshape.609 = bf16[1,2,43,6,2,32,32]{6,5,4,3,2,1,0:T(8,128)(2,1)} reshape(bf16[516,2048]{1,0:T(8,128)(2,1)S(1)} %gather_fusion.1) | data formatting | bytes 4227072 | tf_op jit(solution)/shard_map/reshape | solution.py:12
  34.9 7.3 %slice_bitcast_fusion = (bf16[1,2,43,6,32,32]{5,4,3,2,1,0:T(8,128)(2,1)}, bf16[1,2,43,6,32,32]{5,4,3,2,1,0:T(8,128)(2,1)}) fusion(bf16[1,2,43,6,2,32,32]{6,5,4,3,2,1,0:T(8,128)(2,1)} %reshape.609), kind=kLoop, calls=%fused_computation.14 | loop fusion | bytes 4227072 | tf_op jit(solution)/shard_map/squeeze | solution.py:14
  42.2 1.5 %copy-done.3 = bf16[1,2,43,6,2,32,32]{6,5,4,3,2,1,0:T(8,128)(2,1)S(1)} copy-done((bf16[1,2,43,6,2,32,32]{6,5,4,3,2,1,0:T(8,128)(2,1)S(1)}, bf16[1,2,43,6,2,32,32]{6,5,4,3,2,1,0:T(8,128)(2,1)}, u32[]{:S(2)}) %copy-start.3) | copy-done | bytes 2113560
  43.8 2.5 %fusion.70 = bf16[1,2,43,6,32,32]{5,4,3,2,1,0:T(8,128)(2,1)} fusion(bf16[1,2,43,6,2,32,32]{6,5,4,3,2,1,0:T(8,128)(2,1)S(1)} %copy-done.3), kind=kLoop, calls=%fused_computation.115 | loop fusion | flops 528384 | bytes 2113536 | tf_op jit(solution)/shard_map/neg | solution.py:15
  47.0 2.0 %gather_fusion.3 = s32[86]{0:T(128)S(1)} fusion(s32[2,64]{1,0:T(2,128)S(1)} %copy-done.2, s32[86]{0:T(128)S(1)} %reshape.658), kind=kCustom, calls=%fused_computation.5 | custom fusion | bytes 1376 | tf_op jit(solution)/shard_map/jit(take_along_axis)/gather | solution.py:22
  49.2 9.6 %select_reduce_fusion = bf16[2,36,64,32]{2,3,1,0:T(8,128)(2,1)S(1)} fusion(pred[2,36,6]{2,1,0:T(8,128)(4,1)S(1)} %slice_compare_fusion, bf16[1,2,43,6,32,32]{5,4,3,2,1,0:T(8,128)(2,1)} %get-tuple-element.13, bf16[1,2,43,6,32,32]{5,4,3,2,1,0:T(8,128)(2,1)} %get-tuple-element.12, bf16[1,2,43,6,32,32]{5,4,3,2,1,0:T(8,128)(2,1)} %fusion.70, ...), kind=kOutput, calls=%fused_computation.13 | convolution fusion | flops 129024000 | bytes 3473840 | tf_op jit(solution)/shard_map/easkij,eajc->easkic/dot_general | solution.py:51
  58.8 2.7 %collective-permute-start.1 = (bf16[1,2,2048]{2,1,0:T(2,128)(2,1)S(1)}, bf16[1,2,2048]{2,1,0:T(2,128)(2,1)S(1)}, u32[]{:S(2)}, u32[]{:S(2)}) collective-permute-start(bf16[1,2,2048]{2,1,0:T(2,128)(2,1)S(1)} %collective-permute-done), channel_id=1, source_target_pairs={{0,1},{1,2},{2,3},{3,4},{4,5},{5,6},{6,7},{7,0},{8,9},{9,10},{10,1... | collective-permute-start | bytes 24584 | tf_op jit(solution)/shard_map/ppermute | solution.py:31
  61.5 1.6 %collective-permute-done.1 = bf16[1,2,2048]{2,1,0:T(2,128)(2,1)S(1)} collective-permute-done((bf16[1,2,2048]{2,1,0:T(2,128)(2,1)S(1)}, bf16[1,2,2048]{2,1,0:T(2,128)(2,1)S(1)}, u32[]{:S(2)}, u32[]{:S(2)}) %collective-permute-start.1) | collective-permute-done | bytes 8224 | tf_op jit(solution)/shard_map/ppermute | solution.py:31
  63.2 3.9 %collective-permute-done.2 = bf16[1,2,2048]{2,1,0:T(2,128)(2,1)S(1)} collective-permute-done((bf16[1,2,2048]{2,1,0:T(2,128)(2,1)S(1)}, bf16[1,2,2048]{2,1,0:T(2,128)(2,1)S(1)}, u32[]{:S(2)}, u32[]{:S(2)}) %collective-permute-start.2) | collective-permute-done | bytes 8224 | tf_op jit(solution)/shard_map/ppermute | solution.py:31
  67.1 4.0 %collective-permute-done.3 = bf16[1,2,2048]{2,1,0:T(2,128)(2,1)S(1)} collective-permute-done((bf16[1,2,2048]{2,1,0:T(2,128)(2,1)S(1)}, bf16[1,2,2048]{2,1,0:T(2,128)(2,1)S(1)}, u32[]{:S(2)}, u32[]{:S(2)}) %collective-permute-start.3) | collective-permute-done | bytes 8224 | tf_op jit(solution)/shard_map/ppermute | solution.py:31
  71.1 3.9 %collective-permute-done.4 = bf16[1,2,2048]{2,1,0:T(2,128)(2,1)S(1)} collective-permute-done((bf16[1,2,2048]{2,1,0:T(2,128)(2,1)S(1)}, bf16[1,2,2048]{2,1,0:T(2,128)(2,1)S(1)}, u32[]{:S(2)}, u32[]{:S(2)}) %collective-permute-start.4) | collective-permute-done | bytes 8224 | tf_op jit(solution)/shard_map/ppermute | solution.py:31
  75.0 0.6 fusion.73
  75.7 3.3 %collective-permute-done.5 = bf16[1,2,2048]{2,1,0:T(2,128)(2,1)S(1)} collective-permute-done((bf16[1,2,2048]{2,1,0:T(2,128)(2,1)S(1)}, bf16[1,2,2048]{2,1,0:T(2,128)(2,1)S(1)}, u32[]{:S(2)}, u32[]{:S(2)}) %collective-permute-start.5) | collective-permute-done | bytes 8224 | tf_op jit(solution)/shard_map/ppermute | solution.py:31
  79.0 3.9 %collective-permute-done.6 = bf16[1,2,2048]{2,1,0:T(2,128)(2,1)S(1)} collective-permute-done((bf16[1,2,2048]{2,1,0:T(2,128)(2,1)S(1)}, bf16[1,2,2048]{2,1,0:T(2,128)(2,1)S(1)}, u32[]{:S(2)}, u32[]{:S(2)}) %collective-permute-start.6) | collective-permute-done | bytes 8224 | tf_op jit(solution)/shard_map/ppermute | solution.py:31
  83.0 0.2 concatenate.105
  83.2 0.8 gather_fusion
  84.1 1.1 reshape.694
  85.2 0.2 copy_select_fusion
  85.4 0.3 slice_bitcast_fusion.2
  85.7 1.0 fusion.8
  86.7 0.8 slice-done.1
  87.5 2.2 %fusion.23 = bf16[2,6,64,32]{2,3,1,0:T(8,128)(2,1)S(1)} fusion(bf16[2,6,6,64,32]{3,4,2,1,0:T(8,128)(2,1)S(1)} %bitcast.110, bf16[1,2,43,6,32,32]{5,4,3,2,1,0:T(8,128)(2,1)} %get-tuple-element.13, bf16[1,2,43,6,32,32]{5,4,3,2,1,0:T(8,128)(2,1)} %get-tuple-element.12, bf16[1,2,43,6,32,32]{5,4,3,2,1,0:T(8,128)(2,1)S(1)} %bitcast.109), kind=kOutput, calls=%fused_computation.36 | convolution fusion | flops 21258240 | bytes 3514368 | tf_op jit(solution)/shard_map/eamnij,eamnjc->eamic/dot_general | solution.py:61
  89.7 1.5 %fusion.27 = bf16[2,64,32]{1,2,0:T(8,128)(2,1)S(1)} fusion(bf16[2,6,64,32]{2,3,1,0:T(8,128)(2,1)S(1)} %fusion.23, bf16[1,2,43,32,32]{4,3,2,1,0:T(8,128)(2,1)S(1)} %get-tuple-element.15, bf16[1,2,43,32,32]{4,3,2,1,0:T(8,128)(2,1)S(1)} %get-tuple-element.14, bf16[1,2,43,32,32]{4,3,2,1,0:T(8,128)(2,1)S(1)} %fusion.69, ...), kind=kOutput, calls=%fused_computation.41 | convolution fusion | flops 7155712 | bytes 3772428 | tf_op jit(solution)/shard_map/eanij,eanjc->eaic/dot_general | solution.py:71
  91.2 0.2 fusion.26
  91.4 1.3 %multiply_subtract_fusion = (f32[1,2,32,32]{2,3,1,0:T(8,128)S(1)}, f32[1,2,32,32]{2,3,1,0:T(8,128)S(1)}) fusion(f32[1,2,64,32]{2,3,1,0:T(8,128)S(1)} %fusion.26, f32[]{:T(128)} %bitcast.33, f32[]{:T(128)} %bitcast), kind=kLoop, calls=%fused_computation.75 | loop fusion | flops 12288 | bytes 32776 | tf_op jit(solution)/shard_map/sub | solution.py:84
  93.0 20.3 %psum.7 = f32[2,2048]{1,0:T(2,128)} all-reduce(f32[2,2048]{1,0:T(2,128)S(1)} %pad_maximum_fusion.8), channel_id=1, replica_groups=mesh['energy'=4,'atom'=8] {'energy'}, use_global_device_ids=true, to_apply=%region_1.3 | all-reduce | flops 4096 | bytes 32768 | tf_op jit(solution)/shard_map/psum | solution.py:87
  (73 shorter events, 3.1 us)
Async XLA Ops:
  0.0 22.1 %copy-start = (bf16[1,64,2048]{2,1,0:T(8,128)(2,1)S(1)}, bf16[1,64,2048]{2,1,0:T(8,128)(2,1)}, u32[]{:S(2)}) copy-start(bf16[1,64,2048]{2,1,0:T(8,128)(2,1)} %param.10) | copy-start | bytes 786436
  0.0 14.2 %copy-start.1 = (s32[2,384]{1,0:T(2,128)S(1)}, s32[2,384]{1,0:T(2,128)}, u32[]{:S(2)}) copy-start(s32[2,384]{1,0:T(2,128)} %param.13) | copy-start | bytes 9220
  0.0 58.8 %collective-permute-start = (bf16[1,2,2048]{2,1,0:T(2,128)(2,1)}, bf16[1,2,2048]{2,1,0:T(2,128)(2,1)S(1)}, u32[]{:S(2)}, u32[]{:S(2)}) collective-permute-start(bf16[1,2,2048]{2,1,0:T(2,128)(2,1)} %param.9), channel_id=1, source_target_pairs={{0,1},{1,2},{2,3},{3,4},{4,5},{5,6},{6,7},{7,0},{8,9},{9,10},{10,1... | collective-permute-start | bytes 24584 | tf_op jit(solution)/shard_map/ppermute | solution.py:31
  34.9 8.9 %copy-start.3 = (bf16[1,2,43,6,2,32,32]{6,5,4,3,2,1,0:T(8,128)(2,1)S(1)}, bf16[1,2,43,6,2,32,32]{6,5,4,3,2,1,0:T(8,128)(2,1)}, u32[]{:S(2)}) copy-start(bf16[1,2,43,6,2,32,32]{6,5,4,3,2,1,0:T(8,128)(2,1)} %reshape.609) | copy-start | bytes 6340612
  43.8 2.5 %copy-start.4 = (bf16[1,2,2048]{2,1,0:T(2,128)(2,1)S(1)}, bf16[1,2,2048]{2,1,0:T(2,128)(2,1)}, u32[]{:S(2)}) copy-start(bf16[1,2,2048]{2,1,0:T(2,128)(2,1)} %param.9) | copy-start | bytes 24580
  43.8 3.2 %copy-start.2 = (s32[2,64]{1,0:T(2,128)S(1)}, s32[2,64]{1,0:T(2,128)}, u32[]{:S(2)}) copy-start(s32[2,64]{1,0:T(2,128)} %param.11) | copy-start | bytes 1540
  49.2 12.3 %copy-start.6 = (s32[2]{0:T(128)S(1)}, s32[2]{0:T(128)}, u32[]{:S(2)}) copy-start(s32[2]{0:T(128)} %param.12) | copy-start | bytes 28
  49.2 25.9 %copy-start.5 = (f32[1,2]{1,0:T(1,128)S(1)}, f32[1,2]{1,0:T(1,128)}, u32[]{:S(2)}) copy-start(f32[1,2]{1,0:T(1,128)} %param.15) | copy-start | bytes 28
  58.8 4.3 %collective-permute-start.1 = (bf16[1,2,2048]{2,1,0:T(2,128)(2,1)S(1)}, bf16[1,2,2048]{2,1,0:T(2,128)(2,1)S(1)}, u32[]{:S(2)}, u32[]{:S(2)}) collective-permute-start(bf16[1,2,2048]{2,1,0:T(2,128)(2,1)S(1)} %collective-permute-done), channel_id=1, source_target_pairs={{0,1},{1,2},{2,3},{3,4},{4,5},{5,6},{6,7},{7,0},{8,9},{9,10},{10,1... | collective-permute-start | bytes 24584 | tf_op jit(solution)/shard_map/ppermute | solution.py:31
  63.1 4.0 %collective-permute-start.2 = (bf16[1,2,2048]{2,1,0:T(2,128)(2,1)S(1)}, bf16[1,2,2048]{2,1,0:T(2,128)(2,1)S(1)}, u32[]{:S(2)}, u32[]{:S(2)}) collective-permute-start(bf16[1,2,2048]{2,1,0:T(2,128)(2,1)S(1)} %collective-permute-done.1), channel_id=1, source_target_pairs={{0,1},{1,2},{2,3},{3,4},{4,5},{5,6},{6,7},{7,0},{8,9},{9,10},{10,1... | collective-permute-start | bytes 24584 | tf_op jit(solution)/shard_map/ppermute | solution.py:31
  67.1 4.0 %collective-permute-start.3 = (bf16[1,2,2048]{2,1,0:T(2,128)(2,1)S(1)}, bf16[1,2,2048]{2,1,0:T(2,128)(2,1)S(1)}, u32[]{:S(2)}, u32[]{:S(2)}) collective-permute-start(bf16[1,2,2048]{2,1,0:T(2,128)(2,1)S(1)} %collective-permute-done.2), channel_id=1, source_target_pairs={{0,1},{1,2},{2,3},{3,4},{4,5},{5,6},{6,7},{7,0},{8,9},{9,10},{10,1... | collective-permute-start | bytes 24584 | tf_op jit(solution)/shard_map/ppermute | solution.py:31
  71.1 4.0 %collective-permute-start.4 = (bf16[1,2,2048]{2,1,0:T(2,128)(2,1)S(1)}, bf16[1,2,2048]{2,1,0:T(2,128)(2,1)S(1)}, u32[]{:S(2)}, u32[]{:S(2)}) collective-permute-start(bf16[1,2,2048]{2,1,0:T(2,128)(2,1)S(1)} %collective-permute-done.3), channel_id=1, source_target_pairs={{0,1},{1,2},{2,3},{3,4},{4,5},{5,6},{6,7},{7,0},{8,9},{9,10},{10,1... | collective-permute-start | bytes 24584 | tf_op jit(solution)/shard_map/ppermute | solution.py:31
  75.0 4.0 %collective-permute-start.5 = (bf16[1,2,2048]{2,1,0:T(2,128)(2,1)S(1)}, bf16[1,2,2048]{2,1,0:T(2,128)(2,1)S(1)}, u32[]{:S(2)}, u32[]{:S(2)}) collective-permute-start(bf16[1,2,2048]{2,1,0:T(2,128)(2,1)S(1)} %collective-permute-done.4), channel_id=1, source_target_pairs={{0,1},{1,2},{2,3},{3,4},{4,5},{5,6},{6,7},{7,0},{8,9},{9,10},{10,1... | collective-permute-start | bytes 24584 | tf_op jit(solution)/shard_map/ppermute | solution.py:31
  79.0 4.0 %collective-permute-start.6 = (bf16[1,2,2048]{2,1,0:T(2,128)(2,1)S(1)}, bf16[1,2,2048]{2,1,0:T(2,128)(2,1)S(1)}, u32[]{:S(2)}, u32[]{:S(2)}) collective-permute-start(bf16[1,2,2048]{2,1,0:T(2,128)(2,1)S(1)} %collective-permute-done.5), channel_id=1, source_target_pairs={{0,1},{1,2},{2,3},{3,4},{4,5},{5,6},{6,7},{7,0},{8,9},{9,10},{10,1... | collective-permute-start | bytes 24584 | tf_op jit(solution)/shard_map/ppermute | solution.py:31
  84.1 2.6 %slice-start = ((s8[4227072]{0:T(1024)(128)(4,1)}), s8[32768]{0:T(1024)(128)(4,1)S(1)}, s32[]{:S(2)}) async-start(s8[4227072]{0:T(1024)(128)(4,1)} %bitcast.108), calls=%async_computation | async-start | bytes 65536
  85.4 2.2 %slice-start.1 = ((s8[4227072]{0:T(1024)(128)(4,1)}), s8[4194304]{0:T(1024)(128)(4,1)S(1)}, s32[]{:S(2)}) async-start(s8[4227072]{0:T(1024)(128)(4,1)} %bitcast.108), calls=%async_computation.1 | async-start | bytes 8388608
